TPU v7x, 512 devices: a whole 4x4x16 slice. The times are simulated.
512 devices in a mesh: grp: 4 (over y), walk: 128 (over x, z, core).
Axes of the slice: x: 4, y: 4, z: 16, core: 2. Of those that a mesh axis runs over, the one named last changes fastest.
Arguments:
- log_grads: float32 [1024, 131072], P('walk', 'grp'), may hold values from -60 to 60, as said below
- energies: float32 [1024], P('walk'), may hold values from -6 to 6
Outputs:
- update: float32 [131072], P(('grp', 'walk'))
Inputs may be any that keep to these rules, and one draw needn't show every extreme that they name: `log_grads`: real-valued gradients, every row and column with its own scale.
All inputs are finite; a program needn't handle non-finite values.
Results may differ from a plain program's by a relative error of at most 0.0003.
Values sent between devices are 32-bit elements; how exact they have to be, the bound alone decides.
No kernel may reach another device: no remote copies, remote signals or barrier semaphores. Data moves between devices by JAX's collectives and lax.ppermute only.
A program may use at most 128 MiB of HBM per device.

v0:
```python
import jax
import jax.numpy as jnp
from jax import lax
from jax.sharding import PartitionSpec as P

WALKERS = 1024
damping = 0.0004


def factor_solve(factor, rhs):
    column = rhs[:, None]
    first = lax.linalg.triangular_solve(factor, column, left_side=True, lower=True)
    second = lax.linalg.triangular_solve(
        factor, first, left_side=True, lower=True, transpose_a=True
    )
    return second[:, 0]


def on_device(log_grads, energies):
    all_energy = lax.all_gather(energies, "walk", axis=0, tiled=True)
    regrouped = lax.all_to_all(log_grads, "walk", split_axis=1, concat_axis=0, tiled=True)
    group_params = regrouped.shape[1] * lax.axis_size("walk")
    total_params = group_params * lax.axis_size("grp")
    root_walkers = jnp.sqrt(jnp.float32(WALKERS))
    column_mean = jnp.mean(regrouped, axis=0, keepdims=True)
    centred = (regrouped - column_mean) / root_walkers
    scaled_energy = (all_energy - jnp.mean(all_energy)) / root_walkers
    local_gram = jnp.dot(centred, centred.T, precision=lax.Precision.HIGHEST)
    identity_mat = jnp.eye(WALKERS, dtype=jnp.float32)
    whole_gram = lax.psum(local_gram, ("grp", "walk"))
    factor = jnp.linalg.cholesky(whole_gram + damping * total_params * identity_mat)
    solved = factor_solve(factor, scaled_energy)
    update = jnp.dot(solved, centred, precision=lax.Precision.HIGHEST)
    return -(total_params / root_walkers) * update


def solution(mesh):
    return jax.shard_map(
        on_device,
        mesh=mesh,
        in_specs=(P("walk", "grp"), P("walk")),
        out_specs=P(("grp", "walk")),
        check_vma=False,
    )
```

profile of v0, /device:TPU:2, one launch (start us, length us, event | category | flops | bytes accessed | tf_op | source)
XLA Modules:
  0.0 932.4 jit_solution(15668519067561449194)
XLA Ops:
  6.5 75.6 %all_to_all.13 = f32[8,128,256]{2,0,1:T(8,128)S(1)} all-to-all(f32[8,128,256]{2,0,1:T(8,128)} %bitcast.329), channel_id=1, replica_groups=mesh['grp'=4,'walk'=128] {'walk'}, dimensions={1} | all-to-all | bytes 2097152 | tf_op jit(solution)/shard_map/all_to_all | solution.py:21
  82.3 5.2 fusion.33
  89.8 208.2 %all-reduce.1 = f32[1024]{0:T(1024)S(1)} all-reduce(f32[1024]{0:T(1024)S(1)} %dynamic-update-slice.47), channel_id=1, replica_groups=mesh['grp'=4,'walk'=128] {'walk'}, use_global_device_ids=true, to_apply=%add.1 | all-reduce | flops 1024 | bytes 8192
  299.2 270.7 %all-reduce.4.cloned.1.call-done = f32[1024,1024]{0,1:T(8,128)} async-done(((f32[1024,1024]{0,1:T(8,128)}), f32[1024,1024]{0,1:T(8,128)}) %all-reduce.4.cloned.1.call-update) | async-done | bytes 4194320 | tf_op jit(solution)/shard_map/psum | solution.py:30
  569.9 4.8 select_add_fusion
  574.7 5.8 copy.4
  580.5 4.5 fusion
  586.9 11.7 %cholesky.222 = f32[128,128]{1,0:T(8,128)S(1)} custom-call(f32[128,128]{1,0:T(8,128)S(1)} %cholesky.577), custom_call_target="Cholesky" | custom-call | tf_op jit(solution)/shard_map/jit(cholesky)/cholesky | solution.py:31
  598.8 9.8 %custom-call.64 = f32[1,128,128]{1,2,0:T(8,128)S(1)} custom-call(f32[1,128,128]{2,1,0:T(8,128)S(1)} %get-tuple-element.40), custom_call_target="InvertDiagBlocksLowerTriangular" | custom-call | tf_op jit(solution)/shard_map/jit(cholesky)/cholesky | solution.py:31
  611.9 11.7 %cholesky.243 = f32[128,128]{1,0:T(8,128)S(1)} custom-call(f32[128,128]{1,0:T(8,128)S(1)} %cholesky.581), custom_call_target="Cholesky" | custom-call | tf_op jit(solution)/shard_map/jit(cholesky)/cholesky | solution.py:31
  623.9 2.5 cholesky.254
  626.4 9.8 %custom-call.65 = f32[1,128,128]{1,2,0:T(8,128)S(1)} custom-call(f32[1,128,128]{2,1,0:T(8,128)S(1)} %get-tuple-element.38), custom_call_target="InvertDiagBlocksLowerTriangular" | custom-call | tf_op jit(solution)/shard_map/jit(cholesky)/cholesky | solution.py:31
  639.0 2.7 convolution_subtract_fusion.1
  641.7 11.7 %cholesky.466 = f32[128,128]{1,0:T(8,128)S(1)} custom-call(f32[128,128]{1,0:T(8,128)S(1)} %cholesky.586), custom_call_target="Cholesky" | custom-call | tf_op jit(solution)/shard_map/jit(cholesky)/cholesky | solution.py:31
  654.2 9.8 %custom-call.66 = f32[1,128,128]{1,2,0:T(8,128)S(1)} custom-call(f32[1,128,128]{2,1,0:T(8,128)S(1)} %get-tuple-element.36), custom_call_target="InvertDiagBlocksLowerTriangular" | custom-call | tf_op jit(solution)/shard_map/jit(cholesky)/cholesky | solution.py:31
  665.3 3.3 convolution_subtract_fusion.2
  668.6 11.7 %cholesky.485 = f32[128,128]{1,0:T(8,128)S(1)} custom-call(f32[128,128]{1,0:T(8,128)S(1)} %cholesky.591), custom_call_target="Cholesky" | custom-call | tf_op jit(solution)/shard_map/jit(cholesky)/cholesky | solution.py:31
  681.1 9.8 %custom-call.67 = f32[1,128,128]{1,2,0:T(8,128)S(1)} custom-call(f32[1,128,128]{2,1,0:T(8,128)S(1)} %get-tuple-element.34), custom_call_target="InvertDiagBlocksLowerTriangular" | custom-call | tf_op jit(solution)/shard_map/jit(cholesky)/cholesky | solution.py:31
  692.0 3.1 convolution_subtract_fusion.3
  695.2 12.1 %cholesky.504 = f32[128,128]{1,0:T(8,128)S(1)} custom-call(f32[128,128]{1,0:T(8,128)S(1)} %cholesky.596), custom_call_target="Cholesky" | custom-call | tf_op jit(solution)/shard_map/jit(cholesky)/cholesky | solution.py:31
  708.1 9.8 %custom-call.68 = f32[1,128,128]{1,2,0:T(8,128)S(1)} custom-call(f32[1,128,128]{2,1,0:T(8,128)S(1)} %get-tuple-element.32), custom_call_target="InvertDiagBlocksLowerTriangular" | custom-call | tf_op jit(solution)/shard_map/jit(cholesky)/cholesky | solution.py:31
  719.0 3.1 convolution_subtract_fusion.4
  722.1 11.7 %cholesky.524 = f32[128,128]{1,0:T(8,128)S(1)} custom-call(f32[128,128]{1,0:T(8,128)S(1)} %cholesky.601), custom_call_target="Cholesky" | custom-call | tf_op jit(solution)/shard_map/jit(cholesky)/cholesky | solution.py:31
  734.6 9.8 %custom-call.69 = f32[1,128,128]{1,2,0:T(8,128)S(1)} custom-call(f32[1,128,128]{2,1,0:T(8,128)S(1)} %get-tuple-element.30), custom_call_target="InvertDiagBlocksLowerTriangular" | custom-call | tf_op jit(solution)/shard_map/jit(cholesky)/cholesky | solution.py:31
  745.4 2.8 convolution_subtract_fusion.5
  748.2 11.7 %cholesky.544 = f32[128,128]{1,0:T(8,128)S(1)} custom-call(f32[128,128]{1,0:T(8,128)S(1)} %cholesky.606), custom_call_target="Cholesky" | custom-call | tf_op jit(solution)/shard_map/jit(cholesky)/cholesky | solution.py:31
  760.7 9.8 %custom-call.70 = f32[1,128,128]{1,2,0:T(8,128)S(1)} custom-call(f32[1,128,128]{2,1,0:T(8,128)S(1)} %get-tuple-element.28), custom_call_target="InvertDiagBlocksLowerTriangular" | custom-call | tf_op jit(solution)/shard_map/jit(cholesky)/cholesky | solution.py:31
  773.6 11.7 %cholesky.562 = f32[128,128]{1,0:T(8,128)S(1)} custom-call(f32[128,128]{1,0:T(8,128)S(1)} %convolution_subtract_fusion.6), custom_call_target="Cholesky" | custom-call | tf_op jit(solution)/shard_map/jit(cholesky)/cholesky | solution.py:31
  795.8 4.8 select_select_fusion
  800.6 23.7 %while.1 = (s32[]{:T(128)}, f32[1024,1024]{0,1:T(8,128)}, s32[8,2]{0,1:T(2,128)S(1)}, f32[8,128,128]{2,1,0:T(8,128)S(1)}, s32[]{:T(128)}) while((s32[]{:T(128)}, f32[1024,1024]{0,1:T(8,128)}, s32[8,2]{0,1:T(2,128)S(1)}, f32[8,128,128]{2,1,0:T(8,128)S(1)}, s32[]{:T(128)}) %tuple.49), condition=%wide.while_cond, body=%wide.while_body.sunk | while | flops 2 | bytes 393329 | solution.py:13
  813.1 2.2 dynamic-slice.8
  824.3 78.8 %custom-call.71 = f32[8,128,128]{1,2,0:T(8,128)S(1)} custom-call(f32[8,128,128]{2,1,0:T(8,128)S(1)} %get-tuple-element.12), custom_call_target="InvertDiagBlocksLowerTriangular" | custom-call | tf_op jit(solution)/shard_map/triangular_solve | solution.py:13
  (157 shorter events, 70.8 us)
Async XLA Ops:
  6.5 563.4 %all-reduce.4.cloned.1.call-start = ((), (), s32[]{:S(2)}) async-start(), calls=%async_computation.1 | async-start | bytes 8388608 | tf_op jit(solution)/shard_map/psum | solution.py:30
  82.3 7.2 copy-start.1
  585.0 1.9 copy-start
Sparse Core Ops, SparseCore 0:
  87.7 482.1 all-reduce.3
where the time goes:
time: 938 us; the launch traced here: 932 us
  blocking collectives  284 us (30%)
  waiting for transfers between devices  271 us (29%)
  other arithmetic  262 us (28%)
  matrix products  53.4 us (6%)
  local copies, waits for them, and re-layouts  42 us (4%)
  between operations  20.3 us (2%)
    psum x1, waiting for transfers between devices, on_device(): whole_gram = lax.psum(local_gram, ('grp', 'walk'))  271 us
    unnamed x1, blocking collectives  208 us
    another operation x30, other arithmetic, on_device(): jnp.linalg.cholesky(whole_gram + damping * total_params * identity_mat)  168 us
    another operation x3, other arithmetic, factor_solve(): lax.linalg.triangular_solve(factor, first, left_side=True, lower=True, tr...  83.6 us
    all_to_all x1, blocking collectives, on_device(): lax.all_to_all(log_grads, 'walk', split_axis=1, concat_axis=0, tiled=True)  75.6 us
    another operation x14, matrix products, on_device(): jnp.linalg.cholesky(whole_gram + damping * total_params * identity_mat)  27 us
    another operation x40, local copies, waits for them, and re-layouts  23.5 us
  transfers between devices with their start and end apart: 1, of which 1 were waited for; matrix products, arithmetic and copies ran while one was open for 0% of the time, Pallas kernels for 0%

commit v1 on v0

--- a/solution.py
+++ b/solution.py
@@ -27,7 +27,7 @@
     scaled_energy = (all_energy - jnp.mean(all_energy)) / root_walkers
     local_gram = jnp.dot(centred, centred.T, precision=lax.Precision.HIGHEST)
     identity_mat = jnp.eye(WALKERS, dtype=jnp.float32)
-    whole_gram = lax.psum(local_gram, ("grp", "walk"))
+    whole_gram = lax.psum(lax.psum(local_gram, "walk"), "grp")
     factor = jnp.linalg.cholesky(whole_gram + damping * total_params * identity_mat)
     solved = factor_solve(factor, scaled_energy)
     update = jnp.dot(solved, centred, precision=lax.Precision.HIGHEST)

time: 938 us -> 1060 us (1.13)
  the two profiles are of different devices: /device:TPU:2 before, /device:TPU:8 now
where the time goes in v1:
time: 1060 us; the launch traced here: 1050 us
  waiting for transfers between devices  350 us (33%)
  blocking collectives  325 us (31%)
  other arithmetic  262 us (25%)
  matrix products  53.3 us (5%)
  local copies, waits for them, and re-layouts  42 us (4%)
  between operations  20.3 us (2%)
    psum x2, waiting for transfers between devices, on_device(): whole_gram = lax.psum(lax.psum(local_gram, 'walk'), 'grp')  350 us
    unnamed x1, blocking collectives  250 us
    another operation x30, other arithmetic, on_device(): jnp.linalg.cholesky(whole_gram + damping * total_params * identity_mat)  168 us
    another operation x3, other arithmetic, factor_solve(): lax.linalg.triangular_solve(factor, first, left_side=True, lower=True, tr...  83.6 us
    all_to_all x1, blocking collectives, on_device(): lax.all_to_all(log_grads, 'walk', split_axis=1, concat_axis=0, tiled=True)  75.4 us
    another operation x14, matrix products, on_device(): jnp.linalg.cholesky(whole_gram + damping * total_params * identity_mat)  27 us
    another operation x40, local copies, waits for them, and re-layouts  23.5 us
  transfers between devices with their start and end apart: 2, of which 1 were waited for; matrix products, arithmetic and copies ran while one was open for 0% of the time, Pallas kernels for 0%

profile of v1, /device:TPU:8, one launch (start us, length us, event | category | flops | bytes accessed | tf_op | source)
XLA Modules:
  0.0 1053.3 jit_solution(9512195640686240654)
XLA Ops:
  6.5 75.4 %all_to_all.13 = f32[8,128,256]{2,0,1:T(8,128)S(1)} all-to-all(f32[8,128,256]{2,0,1:T(8,128)} %bitcast.329), channel_id=1, replica_groups=mesh['grp'=4,'walk'=128] {'walk'}, dimensions={1} | all-to-all | bytes 2097152 | tf_op jit(solution)/shard_map/all_to_all | solution.py:21
  82.1 5.2 fusion.33
  87.4 350.1 %all-reduce.5.cloned.1.call-done = f32[1024,1024]{0,1:T(8,128)} async-done(((f32[1024,1024]{0,1:T(8,128)}), f32[1024,1024]{0,1:T(8,128)}) %all-reduce.5.cloned.1.call-update) | async-done | bytes 4194320 | tf_op jit(solution)/shard_map/psum | solution.py:30
  439.7 249.9 %all-reduce.1 = f32[1024]{0:T(1024)S(1)} all-reduce(f32[1024]{0:T(1024)S(1)} %dynamic-update-slice.47), channel_id=1, replica_groups=mesh['grp'=4,'walk'=128] {'walk'}, use_global_device_ids=true, to_apply=%add.1 | all-reduce | flops 1024 | bytes 8192
  690.8 4.8 select_add_fusion
  695.7 5.8 copy.4
  701.5 4.5 fusion
  707.9 11.7 %cholesky.222 = f32[128,128]{1,0:T(8,128)S(1)} custom-call(f32[128,128]{1,0:T(8,128)S(1)} %cholesky.577), custom_call_target="Cholesky" | custom-call | tf_op jit(solution)/shard_map/jit(cholesky)/cholesky | solution.py:31
  719.7 9.8 custom-call.64
  732.8 11.7 %cholesky.243 = f32[128,128]{1,0:T(8,128)S(1)} custom-call(f32[128,128]{1,0:T(8,128)S(1)} %cholesky.581), custom_call_target="Cholesky" | custom-call | tf_op jit(solution)/shard_map/jit(cholesky)/cholesky | solution.py:31
  744.9 2.5 cholesky.254
  747.4 9.8 custom-call.65
  759.9 2.7 convolution_subtract_fusion.1
  762.6 11.7 %cholesky.466 = f32[128,128]{1,0:T(8,128)S(1)} custom-call(f32[128,128]{1,0:T(8,128)S(1)} %cholesky.586), custom_call_target="Cholesky" | custom-call | tf_op jit(solution)/shard_map/jit(cholesky)/cholesky | solution.py:31
  775.1 9.8 custom-call.66
  786.2 3.3 convolution_subtract_fusion.2
  789.6 11.7 %cholesky.485 = f32[128,128]{1,0:T(8,128)S(1)} custom-call(f32[128,128]{1,0:T(8,128)S(1)} %cholesky.591), custom_call_target="Cholesky" | custom-call | tf_op jit(solution)/shard_map/jit(cholesky)/cholesky | solution.py:31
  802.1 9.8 custom-call.67
  813.0 3.1 convolution_subtract_fusion.3
  816.2 12.1 %cholesky.504 = f32[128,128]{1,0:T(8,128)S(1)} custom-call(f32[128,128]{1,0:T(8,128)S(1)} %cholesky.596), custom_call_target="Cholesky" | custom-call | tf_op jit(solution)/shard_map/jit(cholesky)/cholesky | solution.py:31
  829.0 9.8 custom-call.68
  840.0 3.1 convolution_subtract_fusion.4
  843.0 11.7 %cholesky.524 = f32[128,128]{1,0:T(8,128)S(1)} custom-call(f32[128,128]{1,0:T(8,128)S(1)} %cholesky.601), custom_call_target="Cholesky" | custom-call | tf_op jit(solution)/shard_map/jit(cholesky)/cholesky | solution.py:31
  855.5 9.8 custom-call.69
  866.3 2.8 convolution_subtract_fusion.5
  869.2 11.7 %cholesky.544 = f32[128,128]{1,0:T(8,128)S(1)} custom-call(f32[128,128]{1,0:T(8,128)S(1)} %cholesky.606), custom_call_target="Cholesky" | custom-call | tf_op jit(solution)/shard_map/jit(cholesky)/cholesky | solution.py:31
  881.7 9.8 custom-call.70
  894.5 11.7 %cholesky.562 = f32[128,128]{1,0:T(8,128)S(1)} custom-call(f32[128,128]{1,0:T(8,128)S(1)} %convolution_subtract_fusion.6), custom_call_target="Cholesky" | custom-call | tf_op jit(solution)/shard_map/jit(cholesky)/cholesky | solution.py:31
  916.7 4.8 select_select_fusion
  921.5 23.7 %while.1 = (s32[]{:T(128)}, f32[1024,1024]{0,1:T(8,128)}, s32[8,2]{0,1:T(2,128)S(1)}, f32[8,128,128]{2,1,0:T(8,128)S(1)}, s32[]{:T(128)}) while((s32[]{:T(128)}, f32[1024,1024]{0,1:T(8,128)}, s32[8,2]{0,1:T(2,128)S(1)}, f32[8,128,128]{2,1,0:T(8,128)S(1)}, s32[]{:T(128)}) %tuple.49), condition=%wide.while_cond, body=%wide.while_body.sunk | while | flops 2 | bytes 393329 | solution.py:13
  937.1 2.2 dynamic-slice.8
  945.3 78.8 %custom-call.71 = f32[8,128,128]{1,2,0:T(8,128)S(1)} custom-call(f32[8,128,128]{2,1,0:T(8,128)S(1)} %get-tuple-element.12), custom_call_target="InvertDiagBlocksLowerTriangular" | custom-call | tf_op jit(solution)/shard_map/triangular_solve | solution.py:13
  (160 shorter events, 70.9 us)
Async XLA Ops:
  6.5 430.9 %all-reduce.5.cloned.1.call-start = ((), (), s32[]{:S(2)}) async-start(), calls=%async_computation.1 | async-start | bytes 8388608 | tf_op jit(solution)/shard_map/psum | solution.py:30
  87.3 352.1 %copy-start.1 = (f32[8]{0:T(128)S(1)}, f32[8]{0:T(128)}, u32[]{:S(2)}) copy-start(f32[8]{0:T(128)} %param.3) | copy-start | bytes 100
  87.4 603.5 %all-reduce.7.cloned.1.call-start = ((), (), s32[]{:S(2)}) async-start(), calls=%async_computation.2 | async-start | bytes 8388608 | tf_op jit(solution)/shard_map/psum | solution.py:30
  705.9 1.9 copy-start
Sparse Core Ops, SparseCore 0:
  87.5 349.9 all-reduce.4
  439.9 105.2 all-reduce.6
